TPU v7x, 256 devices: a whole 4x4x8 slice. The times are simulated.
256 devices in a mesh: tm: 16 (over y, x), space: 16 (over z, core).
Axes of the slice: x: 4, y: 4, z: 8, core: 2. Of those that a mesh axis runs over, the one named last changes fastest.
Arguments:
- stored: bfloat16 [16, 288, 128, 128], P('tm', None, 'space'), may hold values from -6 to 6
- snapshot: int32 [16, 256], P('tm'), may hold values from 0 to 287, as said below
- balance_coef: float32 [128, 128], P('space'), may hold values from 0.5 to 2
- sea_mask: int32 [128, 128], P('space'), may hold values 0 or 1
Outputs:
- merged_basis: bfloat16 [256, 3, 128, 128], P('tm', None, 'space')
Inputs may be any that keep to these rules, and one draw needn't show every extreme that they name: `snapshot`: the 256 indices of one group are distinct.
All inputs are finite; a program needn't handle non-finite values. No bound on the sum of `sea_mask` on one device may be relied on, other than what follows from the above.
Results may differ from a plain program's by a relative error of at most 0.04.
Values may be sent and summed in bfloat16 or wider, within the bound.
No kernel may reach another device: no remote copies, remote signals or barrier semaphores. Data moves between devices by JAX's collectives and lax.ppermute only.
A program may use at most 64 MiB of HBM per device.

v0:
```python
import jax
import jax.numpy as jnp
from jax import lax
from jax.sharding import PartitionSpec as P

inv_root2 = 0.7071067811865476


def gathered_total(shard, axis):
    return lax.all_gather(shard, axis).astype(jnp.float32).sum(0)


def with_halo(cells, sides, width):
    for axis, dim in sides:
        count = lax.axis_size(axis)
        ends = count - 1
        head = lax.slice_in_dim(cells, 0, width, axis=dim)
        tail = lax.slice_in_dim(cells, cells.shape[dim] - width, cells.shape[dim], axis=dim)
        cells = jnp.concatenate(
            [
                lax.ppermute(tail, axis, [(i, (i + 1) % count) for i in range(ends)]),
                cells,
                lax.ppermute(head, axis, [((i + 1) % count, i) for i in range(ends)]),
            ],
            axis=dim,
        )
    return cells


def from_partner(shard, axis, stride):
    return lax.ppermute(shard, axis, [(i, i ^ 1 << stride) for i in range(lax.axis_size(axis))])


def balance(padded, balance_coef, sea_float):
    center = padded[:, 1:-1, :]
    values = center.astype(jnp.float32)
    east_cells = jnp.roll(values, -1, axis=2)
    west_cells = jnp.roll(values, 1, axis=2)
    zonal_flow = (-balance_coef * sea_float * (east_cells - west_cells)).astype(jnp.bfloat16)
    wide = padded.astype(jnp.float32)
    merid_flow = (balance_coef * sea_float * (wide[:, 2:, :] - wide[:, :-2, :])).astype(
        jnp.bfloat16
    )
    return jnp.stack([center, zonal_flow, merid_flow], axis=1).reshape(center.shape[0], -1)


def stack_pair(own_basis, other_basis, level_idx):
    own_bit = lax.axis_index("tm") // 2**level_idx % 2
    upper_part = jnp.where(own_bit == 0, own_basis, other_basis)
    lower_part = jnp.where(own_bit == 0, other_basis, own_basis)
    return jnp.concatenate([upper_part, lower_part], axis=0)


def merge_pair(own_basis, other_basis, level_idx, last_level):
    stacked = stack_pair(own_basis, other_basis, level_idx)
    summed = own_basis.astype(jnp.float32) + other_basis.astype(jnp.float32)
    local_mixed = (
        jnp.dot(
            stacked.astype(jnp.float32),
            summed.T,
            precision=lax.Precision.HIGHEST,
            preferred_element_type=jnp.float32,
        )
        * inv_root2
    )
    mixed_cols = gathered_total(local_mixed.astype(jnp.bfloat16), "space").astype(jnp.float32)
    normal = jnp.dot(
        mixed_cols.T,
        mixed_cols,
        precision=lax.Precision.HIGHEST,
        preferred_element_type=jnp.float32,
    )
    factor_low = jnp.linalg.cholesky(normal)
    rotation = (
        jax.scipy.linalg.solve_triangular(factor_low, mixed_cols.T, lower=True) * inv_root2
    ).astype(jnp.bfloat16)
    if last_level:
        member_share = rotation.shape[0] // lax.axis_size("tm")
        rotation = lax.dynamic_slice_in_dim(
            rotation, lax.axis_index("tm") * member_share, member_share, 0
        )
    return jnp.dot(rotation, stacked, preferred_element_type=jnp.float32).astype(jnp.bfloat16)


def body(stored, snapshot, balance_coef, sea_mask):
    sea_float = sea_mask.astype(jnp.float32)
    mean_state = jnp.mean(stored[0].astype(jnp.float32), axis=0)
    picked = jnp.take(stored[0], snapshot[0], axis=0)
    anomaly = ((picked.astype(jnp.float32) - mean_state) * sea_float).astype(jnp.bfloat16)
    padded = with_halo(anomaly, (("space", 1),), 1)
    basis_now = balance(padded, balance_coef, sea_float)
    levels = lax.axis_size("tm").bit_length() - 1
    first_level = 0
    other_padded = from_partner(padded, "tm", 0)
    partner = balance(other_padded, balance_coef, sea_float)
    basis_now = merge_pair(basis_now, partner, 0, levels == 1)
    first_level = 1
    for level_idx in range(first_level, levels):
        partner = from_partner(basis_now, "tm", level_idx)
        basis_now = merge_pair(basis_now, partner, level_idx, level_idx == levels - 1)
    return basis_now.reshape(basis_now.shape[0], 3, stored.shape[2], stored.shape[3])


def solution(mesh):
    placed = (P("tm", None, "space", None), P("tm", None), P("space", None), P("space", None))
    return jax.shard_map(
        body, mesh=mesh, in_specs=placed, out_specs=P("tm", None, "space", None), check_vma=False
    )
```

profile of v0, /device:TPU:1, one launch (start us, length us, event | category | flops | bytes accessed | tf_op | source)
XLA Modules:
  0.0 665.0 jit_solution(3835843025007125799)
XLA Ops:
  67.8 7.3 %fusion.32 = bf16[512,256]{1,0:T(8,128)(2,1)} fusion(f32[256,3072]{0,1:T(8,128)} %bitcast.184, bf16[256,3072]{0,1:T(8,128)(2,1)} %bitcast.194, bf16[256,3072]{0,1:T(8,128)(2,1)} %bitcast.196), kind=kOutput, calls=%fused_computation.52 | convolution fusion | flops 4838391808 | bytes 6553600 | tf_op jit(solution)/shard_map/dot_general | solution.py:58
  75.3 44.2 %all-gather.9.cloned.1.call-done = bf16[8192,256]{1,0:T(8,128)(2,1)} async-done(((bf16[512,256]{1,0:T(8,128)(2,1)}), bf16[8192,256]{1,0:T(8,128)(2,1)}) %all-gather.9.cloned.1.call-update) | async-done | bytes 4194320 | tf_op jit(solution)/shard_map/all_gather | solution.py:10
  123.8 11.7 %cholesky.214 = f32[128,128]{1,0:T(8,128)S(1)} custom-call(f32[128,128]{1,0:T(8,128)S(1)} %cholesky.346), custom_call_target="Cholesky" | custom-call | tf_op jit(solution)/shard_map/jit(cholesky)/cholesky | solution.py:73
  135.6 9.8 %custom-call.17 = f32[1,128,128]{1,2,0:T(8,128)S(1)} custom-call(f32[1,128,128]{2,1,0:T(8,128)S(1)} %get-tuple-element.118), custom_call_target="InvertDiagBlocksLowerTriangular" | custom-call | tf_op jit(solution)/shard_map/jit(cholesky)/cholesky | solution.py:73
  145.9 11.7 %cholesky.231 = f32[128,128]{1,0:T(8,128)S(1)} custom-call(f32[128,128]{1,0:T(8,128)S(1)} %convolution_subtract_fusion.7), custom_call_target="Cholesky" | custom-call | tf_op jit(solution)/shard_map/jit(cholesky)/cholesky | solution.py:73
  164.7 19.7 %custom-call.18 = f32[2,128,128]{1,2,0:T(8,128)S(1)} custom-call(f32[2,128,128]{2,1,0:T(8,128)S(1)} %get-tuple-element.33), custom_call_target="InvertDiagBlocksLowerTriangular" | custom-call | tf_op jit(solution)/shard_map/jit(_solve_triangular)/triangular_solve | solution.py:75
  191.9 34.8 %collective-permute-done.3 = bf16[256,3072]{1,0:T(8,128)(2,1)} collective-permute-done((bf16[256,3072]{1,0:T(8,128)(2,1)}, bf16[256,3072]{1,0:T(8,128)(2,1)}, u32[]{:S(2)}, u32[]{:S(2)}) %collective-permute-start.3) | collective-permute-done | bytes 1572896 | tf_op jit(solution)/shard_map/ppermute | solution.py:31
  235.7 41.2 %all-gather.11.cloned.1.call-done = bf16[8192,256]{1,0:T(8,128)(2,1)} async-done(((bf16[512,256]{1,0:T(8,128)(2,1)}), bf16[8192,256]{1,0:T(8,128)(2,1)}) %all-gather.11.cloned.1.call-update) | async-done | bytes 4194320 | tf_op jit(solution)/shard_map/all_gather | solution.py:10
  281.2 11.7 %cholesky.248 = f32[128,128]{1,0:T(8,128)S(1)} custom-call(f32[128,128]{1,0:T(8,128)S(1)} %cholesky.349), custom_call_target="Cholesky" | custom-call | tf_op jit(solution)/shard_map/jit(cholesky)/cholesky | solution.py:73
  293.0 9.8 %custom-call.19 = f32[1,128,128]{1,2,0:T(8,128)S(1)} custom-call(f32[1,128,128]{2,1,0:T(8,128)S(1)} %get-tuple-element.114), custom_call_target="InvertDiagBlocksLowerTriangular" | custom-call | tf_op jit(solution)/shard_map/jit(cholesky)/cholesky | solution.py:73
  303.3 11.7 %cholesky.265 = f32[128,128]{1,0:T(8,128)S(1)} custom-call(f32[128,128]{1,0:T(8,128)S(1)} %convolution_subtract_fusion.6), custom_call_target="Cholesky" | custom-call | tf_op jit(solution)/shard_map/jit(cholesky)/cholesky | solution.py:73
  322.1 19.7 %custom-call.20 = f32[2,128,128]{1,2,0:T(8,128)S(1)} custom-call(f32[2,128,128]{2,1,0:T(8,128)S(1)} %get-tuple-element.34), custom_call_target="InvertDiagBlocksLowerTriangular" | custom-call | tf_op jit(solution)/shard_map/jit(_solve_triangular)/triangular_solve | solution.py:75
  347.8 34.8 %collective-permute-done.4 = bf16[256,3072]{1,0:T(8,128)(2,1)} collective-permute-done((bf16[256,3072]{1,0:T(8,128)(2,1)}, bf16[256,3072]{1,0:T(8,128)(2,1)}, u32[]{:S(2)}, u32[]{:S(2)}) %collective-permute-start.4) | collective-permute-done | bytes 1572896 | tf_op jit(solution)/shard_map/ppermute | solution.py:31
  391.9 41.0 %all-gather.13.cloned.1.call-done = bf16[8192,256]{1,0:T(8,128)(2,1)} async-done(((bf16[512,256]{1,0:T(8,128)(2,1)}), bf16[8192,256]{1,0:T(8,128)(2,1)}) %all-gather.13.cloned.1.call-update) | async-done | bytes 4194320 | tf_op jit(solution)/shard_map/all_gather | solution.py:10
  437.1 11.7 %cholesky.282 = f32[128,128]{1,0:T(8,128)S(1)} custom-call(f32[128,128]{1,0:T(8,128)S(1)} %cholesky.352), custom_call_target="Cholesky" | custom-call | tf_op jit(solution)/shard_map/jit(cholesky)/cholesky | solution.py:73
  448.8 9.8 %custom-call.21 = f32[1,128,128]{1,2,0:T(8,128)S(1)} custom-call(f32[1,128,128]{2,1,0:T(8,128)S(1)} %get-tuple-element.110), custom_call_target="InvertDiagBlocksLowerTriangular" | custom-call | tf_op jit(solution)/shard_map/jit(cholesky)/cholesky | solution.py:73
  459.1 11.7 %cholesky.299 = f32[128,128]{1,0:T(8,128)S(1)} custom-call(f32[128,128]{1,0:T(8,128)S(1)} %convolution_subtract_fusion.5), custom_call_target="Cholesky" | custom-call | tf_op jit(solution)/shard_map/jit(cholesky)/cholesky | solution.py:73
  477.9 19.7 %custom-call.22 = f32[2,128,128]{1,2,0:T(8,128)S(1)} custom-call(f32[2,128,128]{2,1,0:T(8,128)S(1)} %get-tuple-element.35), custom_call_target="InvertDiagBlocksLowerTriangular" | custom-call | tf_op jit(solution)/shard_map/jit(_solve_triangular)/triangular_solve | solution.py:75
  505.1 34.7 %collective-permute-done.5 = bf16[256,3072]{1,0:T(8,128)(2,1)} collective-permute-done((bf16[256,3072]{1,0:T(8,128)(2,1)}, bf16[256,3072]{1,0:T(8,128)(2,1)}, u32[]{:S(2)}, u32[]{:S(2)}) %collective-permute-start.5) | collective-permute-done | bytes 1572896 | tf_op jit(solution)/shard_map/ppermute | solution.py:31
  548.7 41.5 %all-gather.15.cloned.1.call-done = bf16[8192,256]{1,0:T(8,128)(2,1)} async-done(((bf16[512,256]{1,0:T(8,128)(2,1)}), bf16[8192,256]{1,0:T(8,128)(2,1)}) %all-gather.15.cloned.1.call-update) | async-done | bytes 4194320 | tf_op jit(solution)/shard_map/all_gather | solution.py:10
  594.4 11.7 %cholesky.316 = f32[128,128]{1,0:T(8,128)S(1)} custom-call(f32[128,128]{1,0:T(8,128)S(1)} %cholesky.355), custom_call_target="Cholesky" | custom-call | tf_op jit(solution)/shard_map/jit(cholesky)/cholesky | solution.py:73
  606.2 9.8 %custom-call.23 = f32[1,128,128]{1,2,0:T(8,128)S(1)} custom-call(f32[1,128,128]{2,1,0:T(8,128)S(1)} %get-tuple-element.106), custom_call_target="InvertDiagBlocksLowerTriangular" | custom-call | tf_op jit(solution)/shard_map/jit(cholesky)/cholesky | solution.py:73
  616.5 11.9 %cholesky.333 = f32[128,128]{1,0:T(8,128)S(1)} custom-call(f32[128,128]{1,0:T(8,128)S(1)} %convolution_subtract_fusion.4), custom_call_target="Cholesky" | custom-call | tf_op jit(solution)/shard_map/jit(cholesky)/cholesky | solution.py:73
  634.7 19.7 %custom-call.24 = f32[2,128,128]{1,2,0:T(8,128)S(1)} custom-call(f32[2,128,128]{2,1,0:T(8,128)S(1)} %get-tuple-element.36), custom_call_target="InvertDiagBlocksLowerTriangular" | custom-call | tf_op jit(solution)/shard_map/jit(_solve_triangular)/triangular_solve | solution.py:75
  (189 shorter events, 170.3 us)
Async XLA Ops:
  6.5 113.0 %all-gather.9.cloned.1.call-start = ((), (), s32[]{:S(2)}) async-start(), calls=%async_computation | async-start | bytes 4456448 | tf_op jit(solution)/shard_map/all_gather | solution.py:10
  11.9 8.1 %copy-start = (bf16[256,8,128]{2,1,0:T(8,128)(2,1)}, bf16[256,8,128]{2,1,0:T(8,128)(2,1)S(1)}, u32[]{:S(2)}) copy-start(bf16[256,8,128]{2,1,0:T(8,128)(2,1)S(1)} %gather_fusion) | copy-start | bytes 1572868
  12.4 7.6 %collective-permute-start.1 = (bf16[256,1,128]{2,1,0:T(2,128)(2,1)S(1)}, bf16[256,1,128]{2,1,0:T(2,128)(2,1)S(1)}, u32[]{:S(2)}, u32[]{:S(2)}) collective-permute-start(bf16[256,1,128]{2,1,0:T(2,128)(2,1)S(1)} %get-tuple-element.102), channel_id=1, source_target_pairs={{1,0},{2,1},{3,2},{4,3},{5,4},{6,5},{7,6},{8,7},{9,8},{10,9},{11,1... | collective-permute-start | bytes 196616 | tf_op jit(solution)/shard_map/ppermute | solution.py:23
  17.5 3.9 collective-permute-start
  23.0 17.2 %collective-permute-start.2 = (bf16[256,10,128]{2,0,1:T(8,128)(2,1)}, bf16[256,10,128]{2,0,1:T(8,128)(2,1)}, u32[]{:S(2)}, u32[]{:S(2)}) collective-permute-start(bf16[256,10,128]{2,0,1:T(8,128)(2,1)} %copy.43), channel_id=1, source_target_pairs={{0,16},{16,0},{32,48},{48,32},{64,80},{80,64},{96,112},{112,96},{1... | collective-permute-start | bytes 1966088 | tf_op jit(solution)/shard_map/ppermute | solution.py:31
  25.7 5.9 copy-start.11
  25.7 5.9 copy-start.12
  50.9 2.4 copy-start.1
  51.0 2.4 copy-start.3
  51.0 2.6 copy-start.4
  51.0 2.9 copy-start.5
  51.0 3.3 copy-start.6
  54.2 3.0 copy-start.2
  75.1 201.9 %all-gather.11.cloned.1.call-start = ((), (), s32[]{:S(2)}) async-start(), calls=%async_computation.1 | async-start | bytes 4456448 | tf_op jit(solution)/shard_map/all_gather | solution.py:10
  145.4 40.2 %copy-start.7 = (bf16[256,3,8,128]{0,3,2,1:T(8,128)(2,1)S(1)}, bf16[256,3,8,128]{0,3,2,1:T(8,128)(2,1)}, u32[]{:S(2)}) copy-start(bf16[256,3,8,128]{0,3,2,1:T(8,128)(2,1)} %copy.51) | copy-start | bytes 4718596
  189.2 37.5 %collective-permute-start.3 = (bf16[256,3072]{1,0:T(8,128)(2,1)}, bf16[256,3072]{1,0:T(8,128)(2,1)}, u32[]{:S(2)}, u32[]{:S(2)}) collective-permute-start(bf16[256,3072]{1,0:T(8,128)(2,1)} %convolution_convert_fusion.2), channel_id=1, source_target_pairs={{0,32},{16,48},{32,0},{48,16},{64,96},{80,112},{96,64},{112,80},{1... | collective-permute-start | bytes 4718600 | tf_op jit(solution)/shard_map/ppermute | solution.py:31
  228.8 1.2 copy-start.9
  235.5 197.3 %all-gather.13.cloned.1.call-start = ((), (), s32[]{:S(2)}) async-start(), calls=%async_computation.2 | async-start | bytes 4456448 | tf_op jit(solution)/shard_map/all_gather | solution.py:10
  346.6 36.0 %collective-permute-start.4 = (bf16[256,3072]{1,0:T(8,128)(2,1)}, bf16[256,3072]{1,0:T(8,128)(2,1)}, u32[]{:S(2)}, u32[]{:S(2)}) collective-permute-start(bf16[256,3072]{1,0:T(8,128)(2,1)} %convolution_convert_fusion.1), channel_id=1, source_target_pairs={{0,64},{16,80},{32,96},{48,112},{64,0},{80,16},{96,32},{112,48},{1... | collective-permute-start | bytes 4718600 | tf_op jit(solution)/shard_map/ppermute | solution.py:31
  384.6 1.2 copy-start.10
  391.3 198.8 %all-gather.15.cloned.1.call-start = ((), (), s32[]{:S(2)}) async-start(), calls=%async_computation.3 | async-start | bytes 4456448 | tf_op jit(solution)/shard_map/all_gather | solution.py:10
  502.4 37.5 %collective-permute-start.5 = (bf16[256,3072]{1,0:T(8,128)(2,1)}, bf16[256,3072]{1,0:T(8,128)(2,1)}, u32[]{:S(2)}, u32[]{:S(2)}) collective-permute-start(bf16[256,3072]{1,0:T(8,128)(2,1)} %convolution_convert_fusion), channel_id=1, source_target_pairs={{0,128},{16,144},{32,160},{48,176},{64,192},{80,208},{96,224},{112... | collective-permute-start | bytes 4718600 | tf_op jit(solution)/shard_map/ppermute | solution.py:31
  542.0 1.2 copy-start.8
Sparse Core Ops, SparseCore 0:
  75.2 44.3 all-gather.8
  235.6 41.2 all-gather.10
  391.5 41.2 all-gather.12
  548.8 41.2 all-gather.14
where the time goes:
time: 669 us; the launch traced here: 665 us
  waiting for transfers between devices  281 us (42%)
  other arithmetic  252 us (38%)
  local copies, waits for them, and re-layouts  49.5 us (7%)
  matrix products  47.2 us (7%)
  between operations  19.2 us (3%)
  starting transfers between devices  15.8 us (2%)
    all_gather x4, waiting for transfers between devices, gathered_total(): return lax.all_gather(shard, axis).astype(jnp.float32).sum(0)  168 us
    another operation x28, other arithmetic, merge_pair(): factor_low = jnp.linalg.cholesky(normal)  139 us
    ppermute x4, waiting for transfers between devices, from_partner(): lax.ppermute(shard, axis, [(i, i ^ 1 << stride) for i in range(lax.axis_s...  111 us
    another operation x9, other arithmetic, merge_pair(): jax.scipy.linalg.solve_triangular(factor_low, mixed_cols.T, lower=True)  78.8 us
    dot_general x4, matrix products, merge_pair(): jnp.dot(stacked.astype(jnp.float32), summed.T, precision=lax.Precision.HI...  23.8 us
    another operation x29, local copies, waits for them, and re-layouts, merge_pair(): jax.scipy.linalg.solve_triangular(factor_low, mixed_cols.T, lower=True)  15.9 us
  transfers between devices with their start and end apart: 10, of which 10 were waited for; matrix products, arithmetic and copies ran while one was open for 1% of the time, Pallas kernels for 0%

commit v1 on v0

--- a/solution.py
+++ b/solution.py
@@ -53,17 +53,10 @@
 
 def merge_pair(own_basis, other_basis, level_idx, last_level):
     stacked = stack_pair(own_basis, other_basis, level_idx)
-    summed = own_basis.astype(jnp.float32) + other_basis.astype(jnp.float32)
-    local_mixed = (
-        jnp.dot(
-            stacked.astype(jnp.float32),
-            summed.T,
-            precision=lax.Precision.HIGHEST,
-            preferred_element_type=jnp.float32,
-        )
-        * inv_root2
-    )
-    mixed_cols = gathered_total(local_mixed.astype(jnp.bfloat16), "space").astype(jnp.float32)
+    members = own_basis.shape[0]
+    local_gram = jnp.dot(stacked, stacked.T, preferred_element_type=jnp.float32)
+    local_mixed = (local_gram[:, :members] + local_gram[:, members:]) * inv_root2
+    mixed_cols = lax.psum(local_mixed, "space")
     normal = jnp.dot(
         mixed_cols.T,
         mixed_cols,

time: 669 us -> 914 us (1.37)
  waiting for transfers between devices: 281 us -> 557 us
  matrix products: 47.2 us -> 31.5 us
  other arithmetic: 252 us -> 242 us
    psum x0 -> x4, waiting for transfers between devices: none -> 445 us  [merge_pair(): mixed_cols = lax.psum(local_mixed, 'space')]
    all_gather x4 -> x0, waiting for transfers between devices: 168 us -> none  [gathered_total(): return lax.all_gather(shard, axis).astype(jnp.float32).sum(0)]
    dot_general x4, matrix products: 23.8 us -> 9.25 us  [merge_pair(): local_gram = jnp.dot(stacked, stacked.T, preferred_element_type=jnp.float32)]
    reduce_sum x4 -> x0, other arithmetic: 11.3 us -> none  [gathered_total(): return lax.all_gather(shard, axis).astype(jnp.float32).sum(0)]
where the time goes in v1:
time: 914 us; the launch traced here: 906 us
  waiting for transfers between devices  557 us (61%)
  other arithmetic  242 us (26%)
  local copies, waits for them, and re-layouts  40.6 us (4%)
  matrix products  31.5 us (3%)
  between operations  19.2 us (2%)
  starting transfers between devices  15.8 us (2%)
    psum x4, waiting for transfers between devices, merge_pair(): mixed_cols = lax.psum(local_mixed, 'space')  445 us
    another operation x28, other arithmetic, merge_pair(): factor_low = jnp.linalg.cholesky(normal)  139 us
    ppermute x4, waiting for transfers between devices, from_partner(): lax.ppermute(shard, axis, [(i, i ^ 1 << stride) for i in range(lax.axis_s...  110 us
    another operation x9, other arithmetic, merge_pair(): jax.scipy.linalg.solve_triangular(factor_low, mixed_cols.T, lower=True)  78.8 us
  transfers between devices with their start and end apart: 10, of which 10 were waited for; matrix products, arithmetic and copies ran while one was open for 1% of the time, Pallas kernels for 0%

profile of v1, /device:TPU:1, one launch (start us, length us, event | category | flops | bytes accessed | tf_op | source)
XLA Modules:
  0.0 906.3 jit_solution(1723753065468144391)
XLA Ops:
  33.1 7.0 collective-permute-done.2
  66.3 112.4 %all-reduce.6.cloned.1.call-done = f32[512,256]{1,0:T(8,128)} async-done(((f32[512,256]{1,0:T(8,128)}), f32[512,256]{1,0:T(8,128)}) %all-reduce.6.cloned.1.call-update) | async-done | bytes 524304 | tf_op jit(solution)/shard_map/psum | solution.py:59
  181.2 11.7 %cholesky.214 = f32[128,128]{1,0:T(8,128)S(1)} custom-call(f32[128,128]{1,0:T(8,128)S(1)} %cholesky.346), custom_call_target="Cholesky" | custom-call | tf_op jit(solution)/shard_map/jit(cholesky)/cholesky | solution.py:66
  193.0 9.8 %custom-call.17 = f32[1,128,128]{1,2,0:T(8,128)S(1)} custom-call(f32[1,128,128]{2,1,0:T(8,128)S(1)} %get-tuple-element.118), custom_call_target="InvertDiagBlocksLowerTriangular" | custom-call | tf_op jit(solution)/shard_map/jit(cholesky)/cholesky | solution.py:66
  203.3 11.7 %cholesky.231 = f32[128,128]{1,0:T(8,128)S(1)} custom-call(f32[128,128]{1,0:T(8,128)S(1)} %convolution_subtract_fusion.7), custom_call_target="Cholesky" | custom-call | tf_op jit(solution)/shard_map/jit(cholesky)/cholesky | solution.py:66
  222.2 19.7 %custom-call.18 = f32[2,128,128]{1,2,0:T(8,128)S(1)} custom-call(f32[2,128,128]{2,1,0:T(8,128)S(1)} %get-tuple-element.33), custom_call_target="InvertDiagBlocksLowerTriangular" | custom-call | tf_op jit(solution)/shard_map/jit(_solve_triangular)/triangular_solve | solution.py:68
  247.2 34.2 %collective-permute-done.3 = bf16[256,3072]{1,0:T(8,128)(2,1)} collective-permute-done((bf16[256,3072]{1,0:T(8,128)(2,1)S(1)}, bf16[256,3072]{1,0:T(8,128)(2,1)}, u32[]{:S(2)}, u32[]{:S(2)}) %collective-permute-start.3) | collective-permute-done | bytes 1572896 | tf_op jit(solution)/shard_map/ppermute | solution.py:31
  286.4 110.8 %all-reduce.8.cloned.1.call-done = f32[512,256]{1,0:T(8,128)} async-done(((f32[512,256]{1,0:T(8,128)}), f32[512,256]{1,0:T(8,128)}) %all-reduce.8.cloned.1.call-update) | async-done | bytes 524304 | tf_op jit(solution)/shard_map/psum | solution.py:59
  399.6 11.7 %cholesky.248 = f32[128,128]{1,0:T(8,128)S(1)} custom-call(f32[128,128]{1,0:T(8,128)S(1)} %cholesky.349), custom_call_target="Cholesky" | custom-call | tf_op jit(solution)/shard_map/jit(cholesky)/cholesky | solution.py:66
  411.4 9.8 %custom-call.19 = f32[1,128,128]{1,2,0:T(8,128)S(1)} custom-call(f32[1,128,128]{2,1,0:T(8,128)S(1)} %get-tuple-element.114), custom_call_target="InvertDiagBlocksLowerTriangular" | custom-call | tf_op jit(solution)/shard_map/jit(cholesky)/cholesky | solution.py:66
  421.7 11.7 %cholesky.265 = f32[128,128]{1,0:T(8,128)S(1)} custom-call(f32[128,128]{1,0:T(8,128)S(1)} %convolution_subtract_fusion.6), custom_call_target="Cholesky" | custom-call | tf_op jit(solution)/shard_map/jit(cholesky)/cholesky | solution.py:66
  440.2 19.7 %custom-call.20 = f32[2,128,128]{1,2,0:T(8,128)S(1)} custom-call(f32[2,128,128]{2,1,0:T(8,128)S(1)} %get-tuple-element.34), custom_call_target="InvertDiagBlocksLowerTriangular" | custom-call | tf_op jit(solution)/shard_map/jit(_solve_triangular)/triangular_solve | solution.py:68
  464.7 34.4 %collective-permute-done.4 = bf16[256,3072]{1,0:T(8,128)(2,1)} collective-permute-done((bf16[256,3072]{1,0:T(8,128)(2,1)}, bf16[256,3072]{1,0:T(8,128)(2,1)}, u32[]{:S(2)}, u32[]{:S(2)}) %collective-permute-start.4) | collective-permute-done | bytes 1572896 | tf_op jit(solution)/shard_map/ppermute | solution.py:31
  504.4 110.5 %all-reduce.10.cloned.1.call-done = f32[512,256]{1,0:T(8,128)} async-done(((f32[512,256]{1,0:T(8,128)}), f32[512,256]{1,0:T(8,128)}) %all-reduce.10.cloned.1.call-update) | async-done | bytes 524304 | tf_op jit(solution)/shard_map/psum | solution.py:59
  617.4 11.7 %cholesky.282 = f32[128,128]{1,0:T(8,128)S(1)} custom-call(f32[128,128]{1,0:T(8,128)S(1)} %cholesky.352), custom_call_target="Cholesky" | custom-call | tf_op jit(solution)/shard_map/jit(cholesky)/cholesky | solution.py:66
  629.1 9.8 %custom-call.21 = f32[1,128,128]{1,2,0:T(8,128)S(1)} custom-call(f32[1,128,128]{2,1,0:T(8,128)S(1)} %get-tuple-element.110), custom_call_target="InvertDiagBlocksLowerTriangular" | custom-call | tf_op jit(solution)/shard_map/jit(cholesky)/cholesky | solution.py:66
  639.4 11.7 %cholesky.299 = f32[128,128]{1,0:T(8,128)S(1)} custom-call(f32[128,128]{1,0:T(8,128)S(1)} %convolution_subtract_fusion.5), custom_call_target="Cholesky" | custom-call | tf_op jit(solution)/shard_map/jit(cholesky)/cholesky | solution.py:66
  657.9 19.7 %custom-call.22 = f32[2,128,128]{1,2,0:T(8,128)S(1)} custom-call(f32[2,128,128]{2,1,0:T(8,128)S(1)} %get-tuple-element.35), custom_call_target="InvertDiagBlocksLowerTriangular" | custom-call | tf_op jit(solution)/shard_map/jit(_solve_triangular)/triangular_solve | solution.py:68
  684.0 34.4 %collective-permute-done.5 = bf16[256,3072]{1,0:T(8,128)(2,1)} collective-permute-done((bf16[256,3072]{1,0:T(8,128)(2,1)}, bf16[256,3072]{1,0:T(8,128)(2,1)}, u32[]{:S(2)}, u32[]{:S(2)}) %collective-permute-start.5) | collective-permute-done | bytes 1572896 | tf_op jit(solution)/shard_map/ppermute | solution.py:31
  723.2 111.0 %all-reduce.12.cloned.1.call-done = f32[512,256]{1,0:T(8,128)} async-done(((f32[512,256]{1,0:T(8,128)}), f32[512,256]{1,0:T(8,128)}) %all-reduce.12.cloned.1.call-update) | async-done | bytes 524304 | tf_op jit(solution)/shard_map/psum | solution.py:59
  836.6 11.7 %cholesky.316 = f32[128,128]{1,0:T(8,128)S(1)} custom-call(f32[128,128]{1,0:T(8,128)S(1)} %cholesky.355), custom_call_target="Cholesky" | custom-call | tf_op jit(solution)/shard_map/jit(cholesky)/cholesky | solution.py:66
  848.4 9.8 %custom-call.23 = f32[1,128,128]{1,2,0:T(8,128)S(1)} custom-call(f32[1,128,128]{2,1,0:T(8,128)S(1)} %get-tuple-element.106), custom_call_target="InvertDiagBlocksLowerTriangular" | custom-call | tf_op jit(solution)/shard_map/jit(cholesky)/cholesky | solution.py:66
  858.7 11.9 %cholesky.333 = f32[128,128]{1,0:T(8,128)S(1)} custom-call(f32[128,128]{1,0:T(8,128)S(1)} %convolution_subtract_fusion.4), custom_call_target="Cholesky" | custom-call | tf_op jit(solution)/shard_map/jit(cholesky)/cholesky | solution.py:66
  877.2 19.7 %custom-call.24 = f32[2,128,128]{1,2,0:T(8,128)S(1)} custom-call(f32[2,128,128]{2,1,0:T(8,128)S(1)} %get-tuple-element.36), custom_call_target="InvertDiagBlocksLowerTriangular" | custom-call | tf_op jit(solution)/shard_map/jit(_solve_triangular)/triangular_solve | solution.py:68
  (201 shorter events, 136.2 us)
Async XLA Ops:
  6.5 172.3 %all-reduce.6.cloned.1.call-start = ((), (), s32[]{:S(2)}) async-start(), calls=%async_computation | async-start | bytes 1048576 | tf_op jit(solution)/shard_map/psum | solution.py:59
  11.9 8.1 copy-start
  12.4 7.6 collective-permute-start.1
  17.5 3.9 collective-permute-start
  23.0 17.1 %collective-permute-start.2 = (bf16[256,10,128]{2,0,1:T(8,128)(2,1)}, bf16[256,10,128]{2,0,1:T(8,128)(2,1)}, u32[]{:S(2)}, u32[]{:S(2)}) collective-permute-start(bf16[256,10,128]{2,0,1:T(8,128)(2,1)} %copy.45), channel_id=1, source_target_pairs={{0,16},{16,0},{32,48},{48,32},{64,80},{80,64},{96,112},{112,96},{1... | collective-permute-start | bytes 1966088 | tf_op jit(solution)/shard_map/ppermute | solution.py:31
  27.1 4.3 copy-start.20
  27.1 4.3 copy-start.21
  50.9 2.4 copy-start.1
  50.9 2.4 copy-start.6
  50.9 2.6 copy-start.7
  50.9 2.9 copy-start.8
  50.9 3.3 copy-start.9
  54.2 3.0 copy-start.10
  66.0 331.2 %all-reduce.8.cloned.1.call-start = ((), (), s32[]{:S(2)}) async-start(), calls=%async_computation.1 | async-start | bytes 1048576 | tf_op jit(solution)/shard_map/psum | solution.py:59
  181.2 60.7 %copy-start.3 = (f32[512,256]{1,0:T(8,128)S(1)}, f32[512,256]{1,0:T(8,128)}, u32[]{:S(2)}) copy-start(f32[512,256]{1,0:T(8,128)} %all-reduce.6.cloned.1.call-done) | copy-start | bytes 1572868
  244.4 2.8 copy-start.19
  244.4 37.0 %collective-permute-start.3 = (bf16[256,3072]{1,0:T(8,128)(2,1)S(1)}, bf16[256,3072]{1,0:T(8,128)(2,1)}, u32[]{:S(2)}, u32[]{:S(2)}) collective-permute-start(bf16[256,3072]{1,0:T(8,128)(2,1)S(1)} %convolution_convert_fusion.2), channel_id=1, source_target_pairs={{0,32},{16,48},{32,0},{48,16},{64,96},{80,112},{96,64},{112,80},{1... | collective-permute-start | bytes 4718600 | tf_op jit(solution)/shard_map/ppermute | solution.py:31
  286.2 328.8 %all-reduce.10.cloned.1.call-start = ((), (), s32[]{:S(2)}) async-start(), calls=%async_computation.2 | async-start | bytes 1048576 | tf_op jit(solution)/shard_map/psum | solution.py:59
  399.6 60.3 %copy-start.4 = (f32[512,256]{1,0:T(8,128)S(1)}, f32[512,256]{1,0:T(8,128)}, u32[]{:S(2)}) copy-start(f32[512,256]{1,0:T(8,128)} %all-reduce.8.cloned.1.call-done) | copy-start | bytes 1572868
  463.5 35.6 %collective-permute-start.4 = (bf16[256,3072]{1,0:T(8,128)(2,1)}, bf16[256,3072]{1,0:T(8,128)(2,1)}, u32[]{:S(2)}, u32[]{:S(2)}) collective-permute-start(bf16[256,3072]{1,0:T(8,128)(2,1)} %convolution_convert_fusion.1), channel_id=1, source_target_pairs={{0,64},{16,80},{32,96},{48,112},{64,0},{80,16},{96,32},{112,48},{1... | collective-permute-start | bytes 4718600 | tf_op jit(solution)/shard_map/ppermute | solution.py:31
  504.0 330.2 %all-reduce.12.cloned.1.call-start = ((), (), s32[]{:S(2)}) async-start(), calls=%async_computation.3 | async-start | bytes 1048576 | tf_op jit(solution)/shard_map/psum | solution.py:59
  617.3 60.3 %copy-start.5 = (f32[512,256]{1,0:T(8,128)S(1)}, f32[512,256]{1,0:T(8,128)}, u32[]{:S(2)}) copy-start(f32[512,256]{1,0:T(8,128)} %all-reduce.10.cloned.1.call-done) | copy-start | bytes 1572868
  681.3 37.1 %collective-permute-start.5 = (bf16[256,3072]{1,0:T(8,128)(2,1)}, bf16[256,3072]{1,0:T(8,128)(2,1)}, u32[]{:S(2)}, u32[]{:S(2)}) collective-permute-start(bf16[256,3072]{1,0:T(8,128)(2,1)} %convolution_convert_fusion), channel_id=1, source_target_pairs={{0,128},{16,144},{32,160},{48,176},{64,192},{80,208},{96,224},{112... | collective-permute-start | bytes 4718600 | tf_op jit(solution)/shard_map/ppermute | solution.py:31
  836.6 60.3 %copy-start.2 = (f32[512,256]{1,0:T(8,128)S(1)}, f32[512,256]{1,0:T(8,128)}, u32[]{:S(2)}) copy-start(f32[512,256]{1,0:T(8,128)} %all-reduce.12.cloned.1.call-done) | copy-start | bytes 1572868
  (8 other events, 13.3 us)
Sparse Core Ops, SparseCore 0:
  66.1 112.6 all-reduce.5
  286.3 110.8 all-reduce.7
  504.1 110.8 all-reduce.9
  723.3 110.8 all-reduce.11

commit v2 on v1

--- a/solution.py
+++ b/solution.py
@@ -8,6 +8,14 @@
 
 def gathered_total(shard, axis):
     return lax.all_gather(shard, axis).astype(jnp.float32).sum(0)
+
+
+def summed_rows(shard, axis):
+    count = lax.axis_size(axis)
+    parts = lax.all_to_all(shard, axis, 0, 0, tiled=True)
+    parts = parts.reshape(count, shard.shape[0] // count, shard.shape[1])
+    own_rows = parts.astype(jnp.float32).sum(0)
+    return lax.all_gather(own_rows, axis, axis=0, tiled=True)
 
 
 def with_halo(cells, sides, width):
@@ -56,7 +64,7 @@
     members = own_basis.shape[0]
     local_gram = jnp.dot(stacked, stacked.T, preferred_element_type=jnp.float32)
     local_mixed = (local_gram[:, :members] + local_gram[:, members:]) * inv_root2
-    mixed_cols = lax.psum(local_mixed, "space")
+    mixed_cols = summed_rows(local_mixed.astype(jnp.bfloat16), "space")
     normal = jnp.dot(
         mixed_cols.T,
         mixed_cols,

time: 914 us -> 590 us (0.65)
  waiting for transfers between devices: 557 us -> 159 us
  blocking collectives: 0 us -> 64.6 us
  starting transfers between devices: 15.8 us -> 41.5 us
  between operations: 19.2 us -> 6.05 us
    psum x4 -> x0, waiting for transfers between devices: 445 us -> none  [merge_pair(): mixed_cols = lax.psum(local_mixed, 'space')]
    all_gather x0 -> x4, blocking collectives: none -> 64.6 us  [summed_rows(): return lax.all_gather(own_rows, axis, axis=0, tiled=True)]
    all_to_all x0 -> x4, waiting for transfers between devices: none -> 46.3 us  [summed_rows(): parts = lax.all_to_all(shard, axis, 0, 0, tiled=True)]
    all_to_all x0 -> x4, starting transfers between devices: none -> 26.4 us  [summed_rows(): parts = lax.all_to_all(shard, axis, 0, 0, tiled=True)]
  transfers between devices with their start and end apart: 10 -> 10, of which waited for: 10 -> 10; matrix products, arithmetic and copies ran while one was open for 1% -> 2% of each run, Pallas kernels for 0% -> 0%
where the time goes in v2:
time: 590 us; the launch traced here: 582 us
  other arithmetic  241 us (41%)
  waiting for transfers between devices  159 us (27%)
  blocking collectives  64.6 us (11%)
  local copies, waits for them, and re-layouts  42 us (7%)
  starting transfers between devices  41.5 us (7%)
  matrix products  25.9 us (4%)
  between operations  6.05 us (1%)
    another operation x28, other arithmetic, merge_pair(): factor_low = jnp.linalg.cholesky(normal)  139 us
    ppermute x4, waiting for transfers between devices, from_partner(): lax.ppermute(shard, axis, [(i, i ^ 1 << stride) for i in range(lax.axis_s...  111 us
    another operation x9, other arithmetic, merge_pair(): jax.scipy.linalg.solve_triangular(factor_low, mixed_cols.T, lower=True)  78.8 us
    all_gather x4, blocking collectives, summed_rows(): return lax.all_gather(own_rows, axis, axis=0, tiled=True)  64.6 us
    all_to_all x4, waiting for transfers between devices, summed_rows(): parts = lax.all_to_all(shard, axis, 0, 0, tiled=True)  46.3 us
    all_to_all x4, starting transfers between devices, summed_rows(): parts = lax.all_to_all(shard, axis, 0, 0, tiled=True)  26.4 us
    another operation x29, local copies, waits for them, and re-layouts, merge_pair(): jax.scipy.linalg.solve_triangular(factor_low, mixed_cols.T, lower=True)  15.7 us
  transfers between devices with their start and end apart: 10, of which 10 were waited for; matrix products, arithmetic and copies ran while one was open for 2% of the time, Pallas kernels for 0%

profile of v2, /device:TPU:1, one launch (start us, length us, event | category | flops | bytes accessed | tf_op | source)
XLA Modules:
  0.0 581.8 jit_solution(10754543844701832138)
XLA Ops:
  67.5 11.6 %all-to-all-done = bf16[16,32,256]{2,1,0:T(8,128)(2,1)S(1)} async-done(((bf16[16,32,256]{2,1,0:T(8,128)(2,1)}), bf16[16,32,256]{2,1,0:T(8,128)(2,1)S(1)}, u32[]{:S(2)}, u32[]{:S(2)}) %all-to-all-start) | async-done | bytes 262176 | tf_op jit(solution)/shard_map/all_to_all | solution.py:15
  79.1 16.1 %all_gather.12 = f32[512,256]{1,0:T(8,128)S(1)} all-gather(f32[32,256]{1,0:T(8,128)S(1)} %convert_reduce_fusion.4), channel_id=1, replica_groups=mesh['tm'=16,'space'=16] {'space'}, dimensions={0}, use_global_device_ids=true | all-gather | bytes 557056 | tf_op jit(solution)/shard_map/all_gather | solution.py:18
  96.6 11.7 %cholesky.214 = f32[128,128]{1,0:T(8,128)S(1)} custom-call(f32[128,128]{1,0:T(8,128)S(1)} %cholesky.346), custom_call_target="Cholesky" | custom-call | tf_op jit(solution)/shard_map/jit(cholesky)/cholesky | solution.py:74
  108.4 9.8 %custom-call.17 = f32[1,128,128]{1,2,0:T(8,128)S(1)} custom-call(f32[1,128,128]{2,1,0:T(8,128)S(1)} %get-tuple-element.118), custom_call_target="InvertDiagBlocksLowerTriangular" | custom-call | tf_op jit(solution)/shard_map/jit(cholesky)/cholesky | solution.py:74
  118.7 11.7 %cholesky.231 = f32[128,128]{1,0:T(8,128)S(1)} custom-call(f32[128,128]{1,0:T(8,128)S(1)} %convolution_subtract_fusion.7), custom_call_target="Cholesky" | custom-call | tf_op jit(solution)/shard_map/jit(cholesky)/cholesky | solution.py:74
  137.4 19.7 %custom-call.18 = f32[2,128,128]{1,2,0:T(8,128)S(1)} custom-call(f32[2,128,128]{2,1,0:T(8,128)S(1)} %get-tuple-element.33), custom_call_target="InvertDiagBlocksLowerTriangular" | custom-call | tf_op jit(solution)/shard_map/jit(_solve_triangular)/triangular_solve | solution.py:76
  162.3 34.7 %collective-permute-done.3 = bf16[256,3072]{1,0:T(8,128)(2,1)} collective-permute-done((bf16[256,3072]{1,0:T(8,128)(2,1)S(1)}, bf16[256,3072]{1,0:T(8,128)(2,1)}, u32[]{:S(2)}, u32[]{:S(2)}) %collective-permute-start.3) | collective-permute-done | bytes 1572896 | tf_op jit(solution)/shard_map/ppermute | solution.py:39
  207.7 11.6 %all-to-all-done.1 = bf16[16,32,256]{2,1,0:T(8,128)(2,1)S(1)} async-done(((bf16[16,32,256]{2,1,0:T(8,128)(2,1)}), bf16[16,32,256]{2,1,0:T(8,128)(2,1)S(1)}, u32[]{:S(2)}, u32[]{:S(2)}) %all-to-all-start.1) | async-done | bytes 262176 | tf_op jit(solution)/shard_map/all_to_all | solution.py:15
  219.4 16.3 %all_gather.13 = f32[512,256]{1,0:T(8,128)S(1)} all-gather(f32[32,256]{1,0:T(8,128)S(1)} %convert_reduce_fusion.3), channel_id=1, replica_groups=mesh['tm'=16,'space'=16] {'space'}, dimensions={0}, use_global_device_ids=true | all-gather | bytes 557056 | tf_op jit(solution)/shard_map/all_gather | solution.py:18
  237.1 11.7 %cholesky.248 = f32[128,128]{1,0:T(8,128)S(1)} custom-call(f32[128,128]{1,0:T(8,128)S(1)} %cholesky.349), custom_call_target="Cholesky" | custom-call | tf_op jit(solution)/shard_map/jit(cholesky)/cholesky | solution.py:74
  259.2 11.7 %cholesky.265 = f32[128,128]{1,0:T(8,128)S(1)} custom-call(f32[128,128]{1,0:T(8,128)S(1)} %convolution_subtract_fusion.6), custom_call_target="Cholesky" | custom-call | tf_op jit(solution)/shard_map/jit(cholesky)/cholesky | solution.py:74
  277.7 19.7 %custom-call.20 = f32[2,128,128]{1,2,0:T(8,128)S(1)} custom-call(f32[2,128,128]{2,1,0:T(8,128)S(1)} %get-tuple-element.34), custom_call_target="InvertDiagBlocksLowerTriangular" | custom-call | tf_op jit(solution)/shard_map/jit(_solve_triangular)/triangular_solve | solution.py:76
  302.3 34.8 %collective-permute-done.4 = bf16[256,3072]{1,0:T(8,128)(2,1)} collective-permute-done((bf16[256,3072]{1,0:T(8,128)(2,1)}, bf16[256,3072]{1,0:T(8,128)(2,1)}, u32[]{:S(2)}, u32[]{:S(2)}) %collective-permute-start.4) | collective-permute-done | bytes 1572896 | tf_op jit(solution)/shard_map/ppermute | solution.py:39
  347.8 11.6 %all-to-all-done.2 = bf16[16,32,256]{2,1,0:T(8,128)(2,1)S(1)} async-done(((bf16[16,32,256]{2,1,0:T(8,128)(2,1)}), bf16[16,32,256]{2,1,0:T(8,128)(2,1)S(1)}, u32[]{:S(2)}, u32[]{:S(2)}) %all-to-all-start.2) | async-done | bytes 262176 | tf_op jit(solution)/shard_map/all_to_all | solution.py:15
  359.5 16.1 %all_gather.14 = f32[512,256]{1,0:T(8,128)S(1)} all-gather(f32[32,256]{1,0:T(8,128)S(1)} %convert_reduce_fusion.2), channel_id=1, replica_groups=mesh['tm'=16,'space'=16] {'space'}, dimensions={0}, use_global_device_ids=true | all-gather | bytes 557056 | tf_op jit(solution)/shard_map/all_gather | solution.py:18
  377.0 11.7 %cholesky.282 = f32[128,128]{1,0:T(8,128)S(1)} custom-call(f32[128,128]{1,0:T(8,128)S(1)} %cholesky.352), custom_call_target="Cholesky" | custom-call | tf_op jit(solution)/shard_map/jit(cholesky)/cholesky | solution.py:74
  399.1 11.7 %cholesky.299 = f32[128,128]{1,0:T(8,128)S(1)} custom-call(f32[128,128]{1,0:T(8,128)S(1)} %convolution_subtract_fusion.5), custom_call_target="Cholesky" | custom-call | tf_op jit(solution)/shard_map/jit(cholesky)/cholesky | solution.py:74
  417.9 19.7 %custom-call.22 = f32[2,128,128]{1,2,0:T(8,128)S(1)} custom-call(f32[2,128,128]{2,1,0:T(8,128)S(1)} %get-tuple-element.35), custom_call_target="InvertDiagBlocksLowerTriangular" | custom-call | tf_op jit(solution)/shard_map/jit(_solve_triangular)/triangular_solve | solution.py:76
  444.0 34.7 %collective-permute-done.5 = bf16[256,3072]{1,0:T(8,128)(2,1)} collective-permute-done((bf16[256,3072]{1,0:T(8,128)(2,1)}, bf16[256,3072]{1,0:T(8,128)(2,1)}, u32[]{:S(2)}, u32[]{:S(2)}) %collective-permute-start.5) | collective-permute-done | bytes 1572896 | tf_op jit(solution)/shard_map/ppermute | solution.py:39
  489.5 11.6 %all-to-all-done.3 = bf16[16,32,256]{2,1,0:T(8,128)(2,1)S(1)} async-done(((bf16[16,32,256]{2,1,0:T(8,128)(2,1)}), bf16[16,32,256]{2,1,0:T(8,128)(2,1)S(1)}, u32[]{:S(2)}, u32[]{:S(2)}) %all-to-all-start.3) | async-done | bytes 262176 | tf_op jit(solution)/shard_map/all_to_all | solution.py:15
  501.1 16.1 %all_gather.15 = f32[512,256]{1,0:T(8,128)S(1)} all-gather(f32[32,256]{1,0:T(8,128)S(1)} %convert_reduce_fusion.1), channel_id=1, replica_groups=mesh['tm'=16,'space'=16] {'space'}, dimensions={0}, use_global_device_ids=true | all-gather | bytes 557056 | tf_op jit(solution)/shard_map/all_gather | solution.py:18
  518.6 11.7 %cholesky.316 = f32[128,128]{1,0:T(8,128)S(1)} custom-call(f32[128,128]{1,0:T(8,128)S(1)} %cholesky.355), custom_call_target="Cholesky" | custom-call | tf_op jit(solution)/shard_map/jit(cholesky)/cholesky | solution.py:74
  540.7 11.7 %cholesky.333 = f32[128,128]{1,0:T(8,128)S(1)} custom-call(f32[128,128]{1,0:T(8,128)S(1)} %convolution_subtract_fusion.4), custom_call_target="Cholesky" | custom-call | tf_op jit(solution)/shard_map/jit(cholesky)/cholesky | solution.py:74
  559.3 19.7 %custom-call.24 = f32[2,128,128]{1,2,0:T(8,128)S(1)} custom-call(f32[2,128,128]{2,1,0:T(8,128)S(1)} %get-tuple-element.36), custom_call_target="InvertDiagBlocksLowerTriangular" | custom-call | tf_op jit(solution)/shard_map/jit(_solve_triangular)/triangular_solve | solution.py:76
  (201 shorter events, 194.0 us)
Async XLA Ops:
  5.3 8.1 %copy-start = (bf16[256,8,128]{2,1,0:T(8,128)(2,1)}, bf16[256,8,128]{2,1,0:T(8,128)(2,1)S(1)}, u32[]{:S(2)}) copy-start(bf16[256,8,128]{2,1,0:T(8,128)(2,1)S(1)} %gather_fusion) | copy-start | bytes 1572868
  5.9 7.6 %collective-permute-start.1 = (bf16[256,1,128]{2,1,0:T(2,128)(2,1)S(1)}, bf16[256,1,128]{2,1,0:T(2,128)(2,1)S(1)}, u32[]{:S(2)}, u32[]{:S(2)}) collective-permute-start(bf16[256,1,128]{2,1,0:T(2,128)(2,1)S(1)} %get-tuple-element.102), channel_id=1, source_target_pairs={{1,0},{2,1},{3,2},{4,3},{5,4},{6,5},{7,6},{8,7},{9,8},{10,9},{11,1... | collective-permute-start | bytes 196616 | tf_op jit(solution)/shard_map/ppermute | solution.py:31
  11.0 3.9 collective-permute-start
  16.5 17.1 %collective-permute-start.2 = (bf16[256,10,128]{2,0,1:T(8,128)(2,1)}, bf16[256,10,128]{2,0,1:T(8,128)(2,1)}, u32[]{:S(2)}, u32[]{:S(2)}) collective-permute-start(bf16[256,10,128]{2,0,1:T(8,128)(2,1)} %copy.41), channel_id=1, source_target_pairs={{0,16},{16,0},{32,48},{48,32},{64,80},{80,64},{96,112},{112,96},{1... | collective-permute-start | bytes 1966088 | tf_op jit(solution)/shard_map/ppermute | solution.py:39
  20.6 4.3 copy-start.16
  20.6 4.3 copy-start.17
  44.3 2.4 copy-start.1
  44.3 2.4 copy-start.2
  44.3 2.6 copy-start.3
  44.3 2.9 copy-start.4
  44.3 3.3 copy-start.5
  47.6 3.0 copy-start.6
  52.9 1.9 copy-start.7
  59.3 19.8 %all-to-all-start = ((bf16[16,32,256]{2,1,0:T(8,128)(2,1)}), bf16[16,32,256]{2,1,0:T(8,128)(2,1)S(1)}, u32[]{:S(2)}, u32[]{:S(2)}) async-start(bf16[16,32,256]{2,1,0:T(8,128)(2,1)} %bitcast.18), calls=%async_computation | async-start | bytes 524288 | tf_op jit(solution)/shard_map/all_to_all | solution.py:15
  159.5 2.8 copy-start.15
  159.5 37.5 %collective-permute-start.3 = (bf16[256,3072]{1,0:T(8,128)(2,1)S(1)}, bf16[256,3072]{1,0:T(8,128)(2,1)}, u32[]{:S(2)}, u32[]{:S(2)}) collective-permute-start(bf16[256,3072]{1,0:T(8,128)(2,1)S(1)} %convolution_convert_fusion.2), channel_id=1, source_target_pairs={{0,32},{16,48},{32,0},{48,16},{64,96},{80,112},{96,64},{112,80},{1... | collective-permute-start | bytes 4718600 | tf_op jit(solution)/shard_map/ppermute | solution.py:39
  199.1 1.8 copy-start.11
  201.7 17.6 %all-to-all-start.1 = ((bf16[16,32,256]{2,1,0:T(8,128)(2,1)}), bf16[16,32,256]{2,1,0:T(8,128)(2,1)S(1)}, u32[]{:S(2)}, u32[]{:S(2)}) async-start(bf16[16,32,256]{2,1,0:T(8,128)(2,1)} %bitcast.25), calls=%async_computation.1 | async-start | bytes 524288 | tf_op jit(solution)/shard_map/all_to_all | solution.py:15
  301.0 36.1 %collective-permute-start.4 = (bf16[256,3072]{1,0:T(8,128)(2,1)}, bf16[256,3072]{1,0:T(8,128)(2,1)}, u32[]{:S(2)}, u32[]{:S(2)}) collective-permute-start(bf16[256,3072]{1,0:T(8,128)(2,1)} %convolution_convert_fusion.1), channel_id=1, source_target_pairs={{0,64},{16,80},{32,96},{48,112},{64,0},{80,16},{96,32},{112,48},{1... | collective-permute-start | bytes 4718600 | tf_op jit(solution)/shard_map/ppermute | solution.py:39
  339.2 1.8 copy-start.13
  341.8 17.6 %all-to-all-start.2 = ((bf16[16,32,256]{2,1,0:T(8,128)(2,1)}), bf16[16,32,256]{2,1,0:T(8,128)(2,1)S(1)}, u32[]{:S(2)}, u32[]{:S(2)}) async-start(bf16[16,32,256]{2,1,0:T(8,128)(2,1)} %bitcast.32), calls=%async_computation.2 | async-start | bytes 524288 | tf_op jit(solution)/shard_map/all_to_all | solution.py:15
  441.1 37.6 %collective-permute-start.5 = (bf16[256,3072]{1,0:T(8,128)(2,1)}, bf16[256,3072]{1,0:T(8,128)(2,1)}, u32[]{:S(2)}, u32[]{:S(2)}) collective-permute-start(bf16[256,3072]{1,0:T(8,128)(2,1)} %convolution_convert_fusion), channel_id=1, source_target_pairs={{0,128},{16,144},{32,160},{48,176},{64,192},{80,208},{96,224},{112... | collective-permute-start | bytes 4718600 | tf_op jit(solution)/shard_map/ppermute | solution.py:39
  480.8 1.8 copy-start.9
  483.4 17.6 %all-to-all-start.3 = ((bf16[16,32,256]{2,1,0:T(8,128)(2,1)}), bf16[16,32,256]{2,1,0:T(8,128)(2,1)S(1)}, u32[]{:S(2)}, u32[]{:S(2)}) async-start(bf16[16,32,256]{2,1,0:T(8,128)(2,1)} %bitcast.39), calls=%async_computation.3 | async-start | bytes 524288 | tf_op jit(solution)/shard_map/all_to_all | solution.py:15
  (4 other events, 5.6 us)

commit v3 on v2

--- a/solution.py
+++ b/solution.py
@@ -59,9 +59,8 @@
     return jnp.concatenate([upper_part, lower_part], axis=0)
 
 
-def merge_pair(own_basis, other_basis, level_idx, last_level):
-    stacked = stack_pair(own_basis, other_basis, level_idx)
-    members = own_basis.shape[0]
+def rotation_of(stacked):
+    members = stacked.shape[0] // 2
     local_gram = jnp.dot(stacked, stacked.T, preferred_element_type=jnp.float32)
     local_mixed = (local_gram[:, :members] + local_gram[:, members:]) * inv_root2
     mixed_cols = summed_rows(local_mixed.astype(jnp.bfloat16), "space")
@@ -72,14 +71,12 @@
         preferred_element_type=jnp.float32,
     )
     factor_low = jnp.linalg.cholesky(normal)
-    rotation = (
+    return (
         jax.scipy.linalg.solve_triangular(factor_low, mixed_cols.T, lower=True) * inv_root2
     ).astype(jnp.bfloat16)
-    if last_level:
-        member_share = rotation.shape[0] // lax.axis_size("tm")
-        rotation = lax.dynamic_slice_in_dim(
-            rotation, lax.axis_index("tm") * member_share, member_share, 0
-        )
+
+
+def rotated(rotation, stacked):
     return jnp.dot(rotation, stacked, preferred_element_type=jnp.float32).astype(jnp.bfloat16)
 
 
@@ -91,14 +88,24 @@
     padded = with_halo(anomaly, (("space", 1),), 1)
     basis_now = balance(padded, balance_coef, sea_float)
     levels = lax.axis_size("tm").bit_length() - 1
-    first_level = 0
     other_padded = from_partner(padded, "tm", 0)
     partner = balance(other_padded, balance_coef, sea_float)
-    basis_now = merge_pair(basis_now, partner, 0, levels == 1)
-    first_level = 1
-    for level_idx in range(first_level, levels):
-        partner = from_partner(basis_now, "tm", level_idx)
-        basis_now = merge_pair(basis_now, partner, level_idx, level_idx == levels - 1)
+    stacked = stack_pair(basis_now, partner, 0)
+    for level_idx in range(levels):
+        if level_idx == levels - 1:
+            rotation = rotation_of(stacked)
+            member_share = rotation.shape[0] // lax.axis_size("tm")
+            rotation = lax.dynamic_slice_in_dim(
+                rotation, lax.axis_index("tm") * member_share, member_share, 0
+            )
+            basis_now = rotated(rotation, stacked)
+        else:
+            partner_stacked = from_partner(stacked, "tm", level_idx + 1)
+            rotation = rotation_of(stacked)
+            partner_rotation = from_partner(rotation, "tm", level_idx + 1)
+            basis_now = rotated(rotation, stacked)
+            partner = rotated(partner_rotation, partner_stacked)
+            stacked = stack_pair(basis_now, partner, level_idx + 1)
     return basis_now.reshape(basis_now.shape[0], 3, stored.shape[2], stored.shape[3])
 
 

time: 590 us -> 512 us (0.87)
  waiting for transfers between devices: 159 us -> 53.2 us
  matrix products: 25.9 us -> 38.3 us
  starting transfers between devices: 41.5 us -> 48.6 us
    ppermute x4 -> x7, waiting for transfers between devices: 111 us -> 20.3 us  [from_partner(): lax.ppermute(shard, axis, [(i, i ^ 1 << stride) for i in range(lax.axis_s...]
    all_to_all x4, waiting for transfers between devices: 46.3 us -> 31 us  [summed_rows(): parts = lax.all_to_all(shard, axis, 0, 0, tiled=True)]
    dot_general x12 -> x15, matrix products: 19.1 us -> 28 us  [the longest x7 16.6 us: rotated(): jnp.dot(rotation, stacked, preferred_element_type=jnp.float32)]
    concatenate x0 -> x3, other arithmetic: none -> 8.39 us  [stack_pair(): return jnp.concatenate([upper_part, lower_part], axis=0)]
    ppermute x4 -> x7, starting transfers between devices: 8.07 us -> 15.2 us  [from_partner(): lax.ppermute(shard, axis, [(i, i ^ 1 << stride) for i in range(lax.axis_s...]
  transfers between devices with their start and end apart: 10 -> 13, of which waited for: 10 -> 10; matrix products, arithmetic and copies ran while one was open for 2% -> 43% of each run, Pallas kernels for 0% -> 0%
where the time goes in v3:
time: 512 us; the launch traced here: 503 us
  other arithmetic  246 us (48%)
  blocking collectives  64.6 us (13%)
  waiting for transfers between devices  53.2 us (10%)
  starting transfers between devices  48.6 us (9%)
  local copies, waits for them, and re-layouts  44.5 us (9%)
  matrix products  38.3 us (7%)
  between operations  6.23 us (1%)
    another operation x28, other arithmetic, rotation_of(): factor_low = jnp.linalg.cholesky(normal)  139 us
    another operation x9, other arithmetic, rotation_of(): jax.scipy.linalg.solve_triangular(factor_low, mixed_cols.T, lower=True)  80.6 us
    all_gather x4, blocking collectives, summed_rows(): return lax.all_gather(own_rows, axis, axis=0, tiled=True)  64.6 us
    all_to_all x4, waiting for transfers between devices, summed_rows(): parts = lax.all_to_all(shard, axis, 0, 0, tiled=True)  31 us
    all_to_all x4, starting transfers between devices, summed_rows(): parts = lax.all_to_all(shard, axis, 0, 0, tiled=True)  26.4 us
    ppermute x7, waiting for transfers between devices, from_partner(): lax.ppermute(shard, axis, [(i, i ^ 1 << stride) for i in range(lax.axis_s...  20.3 us
    another operation x29, local copies, waits for them, and re-layouts, rotation_of(): jax.scipy.linalg.solve_triangular(factor_low, mixed_cols.T, lower=True)  16.7 us
    dot_general x7, matrix products, rotated(): jnp.dot(rotation, stacked, preferred_element_type=jnp.float32)  16.6 us
  transfers between devices with their start and end apart: 13, of which 10 were waited for; matrix products, arithmetic and copies ran while one was open for 43% of the time, Pallas kernels for 0%

profile of v3, /device:TPU:1, one launch (start us, length us, event | category | flops | bytes accessed | tf_op | source)
XLA Modules:
  0.0 502.8 jit_solution(5525073868484869937)
XLA Ops:
  26.5 7.0 %collective-permute-done.2 = bf16[256,10,128]{2,0,1:T(8,128)(2,1)} collective-permute-done((bf16[256,10,128]{2,0,1:T(8,128)(2,1)}, bf16[256,10,128]{2,0,1:T(8,128)(2,1)}, u32[]{:S(2)}, u32[]{:S(2)}) %collective-permute-start.2) | collective-permute-done | bytes 655392 | tf_op jit(solution)/shard_map/ppermute | solution.py:39
  58.9 8.2 %all-to-all-start = ((bf16[16,32,256]{2,1,0:T(8,128)(2,1)}), bf16[16,32,256]{2,1,0:T(8,128)(2,1)S(1)}, u32[]{:S(2)}, u32[]{:S(2)}) async-start(bf16[16,32,256]{2,1,0:T(8,128)(2,1)} %bitcast.18), calls=%async_computation | async-start | bytes 524288 | tf_op jit(solution)/shard_map/all_to_all | solution.py:15
  78.8 16.1 %all_gather.12 = f32[512,256]{1,0:T(8,128)S(1)} all-gather(f32[32,256]{1,0:T(8,128)S(1)} %convert_reduce_fusion.4), channel_id=1, replica_groups=mesh['tm'=16,'space'=16] {'space'}, dimensions={0}, use_global_device_ids=true | all-gather | bytes 557056 | tf_op jit(solution)/shard_map/all_gather | solution.py:18
  97.2 11.7 %cholesky.214 = f32[128,128]{1,0:T(8,128)S(1)} custom-call(f32[128,128]{1,0:T(8,128)S(1)} %cholesky.346), custom_call_target="Cholesky" | custom-call | tf_op jit(solution)/shard_map/jit(cholesky)/cholesky | solution.py:73
  108.9 9.8 %custom-call.17 = f32[1,128,128]{1,2,0:T(8,128)S(1)} custom-call(f32[1,128,128]{2,1,0:T(8,128)S(1)} %get-tuple-element.118), custom_call_target="InvertDiagBlocksLowerTriangular" | custom-call | tf_op jit(solution)/shard_map/jit(cholesky)/cholesky | solution.py:73
  120.9 11.7 %cholesky.231 = f32[128,128]{1,0:T(8,128)S(1)} custom-call(f32[128,128]{1,0:T(8,128)S(1)} %convolution_subtract_fusion.7), custom_call_target="Cholesky" | custom-call | tf_op jit(solution)/shard_map/jit(cholesky)/cholesky | solution.py:73
  141.2 20.5 %custom-call.18 = f32[2,128,128]{1,2,0:T(8,128)S(1)} custom-call(f32[2,128,128]{2,1,0:T(8,128)} %copy-done.14), custom_call_target="InvertDiagBlocksLowerTriangular" | custom-call | tf_op jit(solution)/shard_map/jit(_solve_triangular)/triangular_solve | solution.py:75
  190.4 7.0 %all-to-all-done.1 = bf16[16,32,256]{2,1,0:T(8,128)(2,1)S(1)} async-done(((bf16[16,32,256]{2,1,0:T(8,128)(2,1)}), bf16[16,32,256]{2,1,0:T(8,128)(2,1)S(1)}, u32[]{:S(2)}, u32[]{:S(2)}) %all-to-all-start.1) | async-done | bytes 262176 | tf_op jit(solution)/shard_map/all_to_all | solution.py:15
  197.5 16.3 %all_gather.13 = f32[512,256]{1,0:T(8,128)S(1)} all-gather(f32[32,256]{1,0:T(8,128)S(1)} %convert_reduce_fusion.3), channel_id=1, replica_groups=mesh['tm'=16,'space'=16] {'space'}, dimensions={0}, use_global_device_ids=true | all-gather | bytes 557056 | tf_op jit(solution)/shard_map/all_gather | solution.py:18
  215.2 11.7 %cholesky.248 = f32[128,128]{1,0:T(8,128)S(1)} custom-call(f32[128,128]{1,0:T(8,128)S(1)} %cholesky.349), custom_call_target="Cholesky" | custom-call | tf_op jit(solution)/shard_map/jit(cholesky)/cholesky | solution.py:73
  227.0 9.8 %custom-call.19 = f32[1,128,128]{1,2,0:T(8,128)S(1)} custom-call(f32[1,128,128]{2,1,0:T(8,128)S(1)} %get-tuple-element.114), custom_call_target="InvertDiagBlocksLowerTriangular" | custom-call | tf_op jit(solution)/shard_map/jit(cholesky)/cholesky | solution.py:73
  237.3 11.7 %cholesky.265 = f32[128,128]{1,0:T(8,128)S(1)} custom-call(f32[128,128]{1,0:T(8,128)S(1)} %convolution_subtract_fusion.6), custom_call_target="Cholesky" | custom-call | tf_op jit(solution)/shard_map/jit(cholesky)/cholesky | solution.py:73
  256.2 19.7 %custom-call.20 = f32[2,128,128]{1,2,0:T(8,128)S(1)} custom-call(f32[2,128,128]{2,1,0:T(8,128)S(1)} %get-tuple-element.34), custom_call_target="InvertDiagBlocksLowerTriangular" | custom-call | tf_op jit(solution)/shard_map/jit(_solve_triangular)/triangular_solve | solution.py:75
  308.2 16.1 %all_gather.14 = f32[512,256]{1,0:T(8,128)S(1)} all-gather(f32[32,256]{1,0:T(8,128)S(1)} %convert_reduce_fusion.2), channel_id=1, replica_groups=mesh['tm'=16,'space'=16] {'space'}, dimensions={0}, use_global_device_ids=true | all-gather | bytes 557056 | tf_op jit(solution)/shard_map/all_gather | solution.py:18
  325.7 11.7 %cholesky.282 = f32[128,128]{1,0:T(8,128)S(1)} custom-call(f32[128,128]{1,0:T(8,128)S(1)} %cholesky.352), custom_call_target="Cholesky" | custom-call | tf_op jit(solution)/shard_map/jit(cholesky)/cholesky | solution.py:73
  337.5 9.8 %custom-call.21 = f32[1,128,128]{1,2,0:T(8,128)S(1)} custom-call(f32[1,128,128]{2,1,0:T(8,128)S(1)} %get-tuple-element.110), custom_call_target="InvertDiagBlocksLowerTriangular" | custom-call | tf_op jit(solution)/shard_map/jit(cholesky)/cholesky | solution.py:73
  347.8 11.7 %cholesky.299 = f32[128,128]{1,0:T(8,128)S(1)} custom-call(f32[128,128]{1,0:T(8,128)S(1)} %convolution_subtract_fusion.5), custom_call_target="Cholesky" | custom-call | tf_op jit(solution)/shard_map/jit(cholesky)/cholesky | solution.py:73
  367.0 19.7 %custom-call.22 = f32[2,128,128]{1,2,0:T(8,128)S(1)} custom-call(f32[2,128,128]{2,1,0:T(8,128)S(1)} %get-tuple-element.35), custom_call_target="InvertDiagBlocksLowerTriangular" | custom-call | tf_op jit(solution)/shard_map/jit(_solve_triangular)/triangular_solve | solution.py:75
  408.8 11.6 %all-to-all-done.3 = bf16[16,32,256]{2,1,0:T(8,128)(2,1)S(1)} async-done(((bf16[16,32,256]{2,1,0:T(8,128)(2,1)}), bf16[16,32,256]{2,1,0:T(8,128)(2,1)S(1)}, u32[]{:S(2)}, u32[]{:S(2)}) %all-to-all-start.3) | async-done | bytes 262176 | tf_op jit(solution)/shard_map/all_to_all | solution.py:15
  420.5 16.1 %all_gather.15 = f32[512,256]{1,0:T(8,128)S(1)} all-gather(f32[32,256]{1,0:T(8,128)S(1)} %convert_reduce_fusion.1), channel_id=1, replica_groups=mesh['tm'=16,'space'=16] {'space'}, dimensions={0}, use_global_device_ids=true | all-gather | bytes 557056 | tf_op jit(solution)/shard_map/all_gather | solution.py:18
  438.0 11.7 %cholesky.316 = f32[128,128]{1,0:T(8,128)S(1)} custom-call(f32[128,128]{1,0:T(8,128)S(1)} %cholesky.355), custom_call_target="Cholesky" | custom-call | tf_op jit(solution)/shard_map/jit(cholesky)/cholesky | solution.py:73
  449.7 9.8 %custom-call.23 = f32[1,128,128]{1,2,0:T(8,128)S(1)} custom-call(f32[1,128,128]{2,1,0:T(8,128)S(1)} %get-tuple-element.106), custom_call_target="InvertDiagBlocksLowerTriangular" | custom-call | tf_op jit(solution)/shard_map/jit(cholesky)/cholesky | solution.py:73
  460.0 11.7 %cholesky.333 = f32[128,128]{1,0:T(8,128)S(1)} custom-call(f32[128,128]{1,0:T(8,128)S(1)} %convolution_subtract_fusion.4), custom_call_target="Cholesky" | custom-call | tf_op jit(solution)/shard_map/jit(cholesky)/cholesky | solution.py:73
  479.1 19.7 %custom-call.24 = f32[2,128,128]{1,2,0:T(8,128)S(1)} custom-call(f32[2,128,128]{2,1,0:T(8,128)S(1)} %get-tuple-element.36), custom_call_target="InvertDiagBlocksLowerTriangular" | custom-call | tf_op jit(solution)/shard_map/jit(_solve_triangular)/triangular_solve | solution.py:75
  (213 shorter events, 202.3 us)
Async XLA Ops:
  5.3 8.1 %copy-start.2 = (bf16[256,8,128]{2,1,0:T(8,128)(2,1)}, bf16[256,8,128]{2,1,0:T(8,128)(2,1)S(1)}, u32[]{:S(2)}) copy-start(bf16[256,8,128]{2,1,0:T(8,128)(2,1)S(1)} %gather_fusion) | copy-start | bytes 1572868
  5.9 7.6 %collective-permute-start.1 = (bf16[256,1,128]{2,1,0:T(2,128)(2,1)S(1)}, bf16[256,1,128]{2,1,0:T(2,128)(2,1)S(1)}, u32[]{:S(2)}, u32[]{:S(2)}) collective-permute-start(bf16[256,1,128]{2,1,0:T(2,128)(2,1)S(1)} %get-tuple-element.102), channel_id=1, source_target_pairs={{1,0},{2,1},{3,2},{4,3},{5,4},{6,5},{7,6},{8,7},{9,8},{10,9},{11,1... | collective-permute-start | bytes 196616 | tf_op jit(solution)/shard_map/ppermute | solution.py:31
  11.0 3.9 collective-permute-start
  16.5 17.1 %collective-permute-start.2 = (bf16[256,10,128]{2,0,1:T(8,128)(2,1)}, bf16[256,10,128]{2,0,1:T(8,128)(2,1)}, u32[]{:S(2)}, u32[]{:S(2)}) collective-permute-start(bf16[256,10,128]{2,0,1:T(8,128)(2,1)} %copy.41), channel_id=1, source_target_pairs={{0,16},{16,0},{32,48},{48,32},{64,80},{80,64},{96,112},{112,96},{1... | collective-permute-start | bytes 1966088 | tf_op jit(solution)/shard_map/ppermute | solution.py:39
  19.0 5.9 %copy-start.15 = (s32[8,128]{1,0:T(8,128)S(1)}, s32[8,128]{1,0:T(8,128)}, u32[]{:S(2)}) copy-start(s32[8,128]{1,0:T(8,128)} %param.10) | copy-start | bytes 12292
  19.0 5.9 %copy-start.16 = (f32[8,128]{1,0:T(8,128)S(1)}, f32[8,128]{1,0:T(8,128)}, u32[]{:S(2)}) copy-start(f32[8,128]{1,0:T(8,128)} %param.9) | copy-start | bytes 12292
  43.9 3.7 copy-start.3
  45.2 2.5 copy-start.5
  45.2 2.8 copy-start.6
  45.2 3.1 copy-start.7
  45.2 3.4 copy-start.8
  48.7 3.0 copy-start.9
  56.3 10.8 %copy-start = (bf16[256,3,8,128]{0,3,2,1:T(8,128)(2,1)}, bf16[256,3,8,128]{0,3,2,1:T(8,128)(2,1)S(1)}, u32[]{:S(2)}) copy-start(bf16[256,3,8,128]{0,3,2,1:T(8,128)(2,1)S(1)} %copy.48) | copy-start | bytes 4718596
  58.9 19.8 %all-to-all-start = ((bf16[16,32,256]{2,1,0:T(8,128)(2,1)}), bf16[16,32,256]{2,1,0:T(8,128)(2,1)S(1)}, u32[]{:S(2)}, u32[]{:S(2)}) async-start(bf16[16,32,256]{2,1,0:T(8,128)(2,1)} %bitcast.18), calls=%async_computation | async-start | bytes 524288 | tf_op jit(solution)/shard_map/all_to_all | solution.py:15
  69.1 105.1 %collective-permute-start.4 = (bf16[512,3072]{0,1:T(8,128)(2,1)}, bf16[512,3072]{0,1:T(8,128)(2,1)}, u32[]{:S(2)}, u32[]{:S(2)}) collective-permute-start(bf16[512,3072]{0,1:T(8,128)(2,1)} %pad_maximum_fusion), channel_id=1, source_target_pairs={{0,32},{16,48},{32,0},{48,16},{64,96},{80,112},{96,64},{112,80},{1... | collective-permute-start | bytes 9437192 | tf_op jit(solution)/shard_map/ppermute | solution.py:39
  97.2 70.6 %copy-start.1 = (bf16[256,3,8,128]{0,3,2,1:T(8,128)(2,1)S(1)}, bf16[256,3,8,128]{0,3,2,1:T(8,128)(2,1)}, u32[]{:S(2)}) copy-start(bf16[256,3,8,128]{0,3,2,1:T(8,128)(2,1)} %copy-done) | copy-start | bytes 4718596
  164.9 9.3 %collective-permute-start.3 = (bf16[256,512]{1,0:T(8,128)(2,1)S(1)}, bf16[256,512]{1,0:T(8,128)(2,1)S(1)}, u32[]{:S(2)}, u32[]{:S(2)}) collective-permute-start(bf16[256,512]{1,0:T(8,128)(2,1)S(1)} %fusion.20), channel_id=1, source_target_pairs={{0,32},{16,48},{32,0},{48,16},{64,96},{80,112},{96,64},{112,80},{1... | collective-permute-start | bytes 786440 | tf_op jit(solution)/shard_map/ppermute | solution.py:39
  179.8 17.6 %all-to-all-start.1 = ((bf16[16,32,256]{2,1,0:T(8,128)(2,1)}), bf16[16,32,256]{2,1,0:T(8,128)(2,1)S(1)}, u32[]{:S(2)}, u32[]{:S(2)}) async-start(bf16[16,32,256]{2,1,0:T(8,128)(2,1)} %bitcast.25), calls=%async_computation.1 | async-start | bytes 524288 | tf_op jit(solution)/shard_map/all_to_all | solution.py:15
  189.1 95.9 %collective-permute-start.6 = (bf16[512,3072]{1,0:T(8,128)(2,1)}, bf16[512,3072]{1,0:T(8,128)(2,1)}, u32[]{:S(2)}, u32[]{:S(2)}) collective-permute-start(bf16[512,3072]{1,0:T(8,128)(2,1)} %pad_maximum_fusion.1), channel_id=1, source_target_pairs={{0,64},{16,80},{32,96},{48,112},{64,0},{80,16},{96,32},{112,48},{1... | collective-permute-start | bytes 9437192 | tf_op jit(solution)/shard_map/ppermute | solution.py:39
  277.2 7.8 %collective-permute-start.5 = (bf16[256,512]{1,0:T(8,128)(2,1)S(1)}, bf16[256,512]{1,0:T(8,128)(2,1)S(1)}, u32[]{:S(2)}, u32[]{:S(2)}) collective-permute-start(bf16[256,512]{1,0:T(8,128)(2,1)S(1)} %fusion.21), channel_id=1, source_target_pairs={{0,64},{16,80},{32,96},{48,112},{64,0},{80,16},{96,32},{112,48},{1... | collective-permute-start | bytes 786440 | tf_op jit(solution)/shard_map/ppermute | solution.py:39
  290.5 17.6 %all-to-all-start.2 = ((bf16[16,32,256]{2,1,0:T(8,128)(2,1)}), bf16[16,32,256]{2,1,0:T(8,128)(2,1)S(1)}, u32[]{:S(2)}, u32[]{:S(2)}) async-start(bf16[16,32,256]{2,1,0:T(8,128)(2,1)} %bitcast.32), calls=%async_computation.2 | async-start | bytes 524288 | tf_op jit(solution)/shard_map/all_to_all | solution.py:15
  299.8 97.4 %collective-permute-start.8 = (bf16[512,3072]{1,0:T(8,128)(2,1)}, bf16[512,3072]{1,0:T(8,128)(2,1)}, u32[]{:S(2)}, u32[]{:S(2)}) collective-permute-start(bf16[512,3072]{1,0:T(8,128)(2,1)} %pad_maximum_fusion.2), channel_id=1, source_target_pairs={{0,128},{16,144},{32,160},{48,176},{64,192},{80,208},{96,224},{112... | collective-permute-start | bytes 9437192 | tf_op jit(solution)/shard_map/ppermute | solution.py:39
  387.9 9.3 %collective-permute-start.7 = (bf16[256,512]{1,0:T(8,128)(2,1)S(1)}, bf16[256,512]{1,0:T(8,128)(2,1)S(1)}, u32[]{:S(2)}, u32[]{:S(2)}) collective-permute-start(bf16[256,512]{1,0:T(8,128)(2,1)S(1)} %fusion.22), channel_id=1, source_target_pairs={{0,128},{16,144},{32,160},{48,176},{64,192},{80,208},{96,224},{112... | collective-permute-start | bytes 786440 | tf_op jit(solution)/shard_map/ppermute | solution.py:39
  402.8 17.6 %all-to-all-start.3 = ((bf16[16,32,256]{2,1,0:T(8,128)(2,1)}), bf16[16,32,256]{2,1,0:T(8,128)(2,1)S(1)}, u32[]{:S(2)}, u32[]{:S(2)}) async-start(bf16[16,32,256]{2,1,0:T(8,128)(2,1)} %bitcast.39), calls=%async_computation.3 | async-start | bytes 524288 | tf_op jit(solution)/shard_map/all_to_all | solution.py:15
  (7 other events, 11.5 us)
